TPU v7x, 512 devices: a whole 4x8x8 slice. The times are simulated.
512 devices in a mesh: wall: 4 (over x_lo, core), span: 16 (over y, x_hi), stream: 8 (over z).
Axes of the slice: x: 4 (x_hi: 2, x_lo: 2; x = x_hi * 2 + x_lo), y: 8, z: 8, core: 2. Of those that a mesh axis runs over, the one named last changes fastest.
Arguments:
- right_side: float32 [16, 8, 8, 64, 320], P('span', 'stream', 'wall'), may hold values from -6 to 6
- old_values: float32 [16, 8, 8, 64, 320], P('span', 'stream', 'wall'), may hold values from -6 to 6
- element_library: float32 [8, 320], replicated, as said below
- wall_library: float32 [3, 320, 320], replicated, as said below
- face_library: float32 [4, 320, 320], replicated, may hold values from -0.15625 to 0.15625
- element_index: int32 [16, 8, 8], P('span', 'stream', 'wall'), may hold values from 0 to 7
- wall_faces: int32 [16, 8, 8, 2], P('span', 'stream', 'wall'), may hold values from 0 to 2, as said below
- face_index: int32 [16, 8, 8, 4], P('span', 'stream', 'wall'), may hold values from 0 to 3
Outputs:
- new_values: float32 [16, 8, 8, 64, 320], P('span', 'stream', 'wall')
Inputs may be any that keep to these rules, and one draw needn't show every extreme that they name: On every line wall_faces[..., i, 1] equals wall_faces[..., i + 1, 0] for i < 7. `wall_library`: every block is symmetric positive definite. `element_library`: entries are positive.
All inputs are finite; a program needn't handle non-finite values.
Results may differ from a plain program's by a relative error of at most 0.0003.
Values sent between devices are 32-bit elements; how exact they have to be, the bound alone decides.
No kernel may reach another device: no remote copies, remote signals or barrier semaphores. Data moves between devices by JAX's collectives and lax.ppermute only.
A program may use at most 64 MiB of HBM per device.

v0:
```python
from functools import partial

import jax
import jax.numpy as jnp
from jax import lax
from jax.sharding import PartitionSpec as P

HIGHEST = lax.Precision.HIGHEST


def padded_2(cells, sides, width):
    for axis, dim in sides:
        count = lax.axis_size(axis)
        head = lax.slice_in_dim(cells, 0, width, axis=dim)
        tail = lax.slice_in_dim(cells, cells.shape[dim] - width, cells.shape[dim], axis=dim)
        cells = jnp.concatenate(
            [
                lax.ppermute(tail, axis, [(i, (i + 1) % count) for i in range(count)]),
                cells,
                lax.ppermute(head, axis, [((i + 1) % count, i) for i in range(count)]),
            ],
            axis=dim,
        )
    return cells


def from_behind(value, axis, by):
    length = lax.axis_size(axis)
    pairs = [(i, i + by) for i in range(length) if 0 <= i + by < length]
    return lax.ppermute(value, axis, pairs)


def lower_solve(factor, values):
    return jax.scipy.linalg.solve_triangular(factor, values, lower=True)


def upper_solve(factor, values):
    return jax.scipy.linalg.solve_triangular(factor, values, lower=True, trans=1)


def coupled_sum(index_rows, near_rows, face_library):

    def one_element(per_element):
        index_row, near_now = per_element
        return jnp.einsum("djk,dvk->jv", face_library[index_row], near_now, precision=HIGHEST)

    return lax.map(one_element, (index_rows, near_rows))


def eliminate(
    element_rates, prev_faces, next_faces, residual_t, wall_library, factor_in, carried_in, linked
):
    element_count = element_rates.shape[0]
    link_flags = jnp.ones((element_count,), jnp.float32)
    if not linked:
        link_flags = link_flags.at[0].set(0.0)

    def advance_one(carried_state, per_element):
        factor_prev, carried_prev, unused_pivot = carried_state
        rate_row, prev_face, next_face, residual_row, link_flag = per_element
        coupling = wall_library[prev_face]
        scaled = lower_solve(factor_prev, coupling)
        reduced = lower_solve(factor_prev, carried_prev)
        pivot_now = (
            jnp.diag(rate_row)
            + coupling
            + wall_library[next_face]
            - link_flag * jnp.dot(scaled.T, scaled, precision=HIGHEST)
        )
        carried = residual_row + link_flag * jnp.dot(scaled.T, reduced, precision=HIGHEST)
        factor = jnp.linalg.cholesky(pivot_now)
        return ((factor, carried, pivot_now), (factor, carried))

    start_carry = (factor_in, carried_in, jnp.zeros_like(factor_in))
    last_state, (factors, carries) = lax.scan(
        advance_one, start_carry, (element_rates, prev_faces, next_faces, residual_t, link_flags)
    )
    return (factors, carries, last_state[0], last_state[1], last_state[2])


def substitute(factors, carries, prev_faces, wall_library, term_in):

    def retreat_one(term_next, per_element):
        factor, carried, prev_face = per_element
        solution = upper_solve(factor, lower_solve(factor, carried + term_next))
        return (jnp.dot(wall_library[prev_face], solution, precision=HIGHEST), solution)

    term_first, solutions = lax.scan(
        retreat_one, term_in, (factors, carries, prev_faces), reverse=True
    )
    return (solutions, term_first)


def keep_state(section_state):
    return section_state


def forward_section(
    section_state, element_rates, prev_faces, next_faces, residual_t, wall_library, linked
):
    payload_in = section_state[4]
    unknowns = payload_in.shape[0]
    results = eliminate(
        element_rates,
        prev_faces,
        next_faces,
        residual_t,
        wall_library,
        payload_in[:, :unknowns],
        payload_in[:, unknowns:],
        linked,
    )
    payload_new = jnp.concatenate([results[2], results[3]], axis=1)
    return (results[0], results[1], payload_new, results[4], payload_in)


def backward_section(back_state, factors, carries, prev_faces, wall_library):
    solutions, term_first = substitute(factors, carries, prev_faces, wall_library, back_state[2])
    return (solutions, term_first, back_state[2])


def on_device(
    right_side,
    old_values,
    element_library,
    wall_library,
    face_library,
    element_index,
    wall_faces,
    face_index,
):
    local_side = right_side[0, 0]
    element_count = local_side.shape[0]
    vector_count = local_side.shape[1]
    unknowns = local_side.shape[2]
    padded = padded_2(old_values, (("span", 0), ("stream", 1)), 1)
    near_rows = jnp.stack([padded[0, 1], padded[2, 1], padded[1, 0], padded[1, 2]], axis=1)
    coupled = coupled_sum(face_index[0, 0], near_rows, face_library)
    residual_t = jnp.swapaxes(local_side, 1, 2) - coupled
    library_row_list = jnp.arange(element_library.shape[0], dtype=jnp.int32)
    selector = (element_index[0, 0][:, None] == library_row_list[None, :]).astype(jnp.float32)
    element_rates = jnp.dot(selector, element_library, precision=HIGHEST)
    below_faces = wall_faces[0, 0, :, 0]
    above_faces = wall_faces[0, 0, :, 1]
    wall_position = lax.axis_index("wall")
    wall_count = lax.axis_size("wall")
    identity = jnp.eye(unknowns, dtype=jnp.float32)
    zero_carried = jnp.zeros((unknowns, vector_count), jnp.float32)
    start_payload = jnp.concatenate([identity, zero_carried], axis=1)
    empty_factors = jnp.zeros((element_count, unknowns, unknowns), jnp.float32)
    empty_carries = jnp.zeros((element_count, unknowns, vector_count), jnp.float32)
    section_state = (empty_factors, empty_carries, start_payload, identity, start_payload)
    for section_number in range(wall_count):
        if section_number > 0:
            payload_in = from_behind(section_state[2], "wall", 1)
            section_state = section_state[:4] + (payload_in,)
        advance = partial(
            forward_section,
            element_rates=element_rates,
            prev_faces=below_faces,
            next_faces=above_faces,
            residual_t=residual_t,
            wall_library=wall_library,
            linked=section_number > 0,
        )
        section_state = lax.cond(
            wall_position == section_number, advance, keep_state, section_state
        )
    factors, carries = (section_state[0], section_state[1])
    back_state = (empty_carries, zero_carried, zero_carried)
    for section_number in range(wall_count):
        if section_number > 0:
            term_in = from_behind(back_state[1], "wall", -1)
            back_state = back_state[:2] + (term_in,)
        retreat = partial(
            backward_section,
            factors=factors,
            carries=carries,
            prev_faces=below_faces,
            wall_library=wall_library,
        )
        back_state = lax.cond(
            wall_position == wall_count - 1 - section_number, retreat, keep_state, back_state
        )
    physical = back_state[0]
    return jnp.swapaxes(physical, 1, 2)[None, None]


def solution(mesh):
    placed = (
        P("span", "stream", "wall", None, None),
        P("span", "stream", "wall", None, None),
        P(),
        P(),
        P(),
        P("span", "stream", "wall"),
        P("span", "stream", "wall", None),
        P("span", "stream", "wall", None),
    )
    return jax.shard_map(
        on_device,
        mesh=mesh,
        in_specs=placed,
        out_specs=P("span", "stream", "wall", None, None),
        check_vma=False,
    )
```

profile of v0, /device:TPU:32, one launch (start us, length us, event | category | flops | bytes accessed | tf_op | source)
XLA Modules:
  0.0 1320.7 jit_solution(586580210752087053)
XLA Ops:
  16.7 10.9 collective-permute-start.3
  31.4 9.0 collective-permute-done.3
  46.8 11.4 while.188
  59.9 223.7 %conditional.8 = (f32[2,320,320]{2,1,0:T(8,128)}, f32[2,320,64]{1,2,0:T(8,128)}, f32[320,384]{1,0:T(8,128)}) conditional(s32[]{:T(128)} %convert_element_type.22, f32[320,384]{1,0:T(8,128)} %concatenate.47, (f32[2,320]{1,0:T(2,128)S(1)}, s32[2]{0:T(128)}, f32[3,320,320]{2,1,0:T(8,128)S(1)}, s32[2]{0:T(128)S(1)}, f32[2,320,64]{1,2,0:T(8,128)}, ...), branch_computations={%region_2.3_spmd, %region_3.15_spmd} | conditional | flops 895840576 | bytes 18580134 | solution.py:166
  61.6 207.0 %while.187 = (s32[]{:T(128)}, f32[320,320]{1,0:T(8,128)S(1)}, f32[320,64]{0,1:T(8,128)S(1)}, f32[2,320,320]{2,1,0:T(8,128)}, f32[2,320,64]{1,2,0:T(8,128)}, /*in...) while((s32[]{:T(128)}, f32[320,320]{1,0:T(8,128)S(1)}, ...), condition=%wide.region_11.14_spmd.clone, body=%wide.region_4.13_spmd.clone.sunk | while | flops 895717696 | bytes 13337058 | solution.py:75
  66.2 29.5 %custom-call.135 = f32[3,128,128]{1,2,0:T(8,128)S(1)} custom-call(f32[3,128,128]{2,1,0:T(8,128)S(1)} %pad_maximum_fusion.63), custom_call_target="InvertDiagBlocksLowerTriangular" | custom-call | tf_op jit(solution)/shard_map/cond/branch_1_fun/while/body/eval_jaxpr/jit(_solve_triangular)/triangular_solve | solution.py:34
  111.3 11.7 cholesky.1249
  123.1 9.8 custom-call.136
  133.4 11.7 cholesky.1252
  147.1 9.8 custom-call.137
  169.5 29.5 %custom-call.135 = f32[3,128,128]{1,2,0:T(8,128)S(1)} custom-call(f32[3,128,128]{2,1,0:T(8,128)S(1)} %pad_maximum_fusion.63), custom_call_target="InvertDiagBlocksLowerTriangular" | custom-call | tf_op jit(solution)/shard_map/cond/branch_1_fun/while/body/eval_jaxpr/jit(_solve_triangular)/triangular_solve | solution.py:34
  214.6 11.7 cholesky.1249
  226.4 9.8 custom-call.136
  236.7 11.7 cholesky.1252
  250.4 9.8 custom-call.137
  286.7 14.0 %conditional.9 = ((f32[2,320,320]{2,1,0:T(8,128)}, f32[2,320,64]{1,2,0:T(8,128)}, f32[320,384]{1,0:T(8,128)})) conditional(s32[]{:T(128)} %convert_element_type.23, (f32[2,320,320]{2,1,0:T(8,128)}, f32[2,320,64]{1,2,0:T(8,128)}, f32[320,384]{1,0:T(8,128)}) %conditional.8, (f32[320,384]{1,0:T(8,128)S(1)}, f32[2,320]{1,0:T(2,128)S(1)}, s32[2]{0:T(128)}, ...), branch_computations={%region_12.16_spmd, %region_13.19_spmd} | conditional | flops 895697216 | bytes 29786412 | solution.py:166
  300.7 214.3 %collective-permute-start.5 = (f32[320,384]{1,0:T(8,128)}, f32[320,384]{1,0:T(8,128)}, u32[]{:S(2)}, u32[]{:S(2)}) collective-permute-start(f32[320,384]{1,0:T(8,128)} %get-tuple-element.1013), channel_id=1, source_target_pairs={{0,128},{128,256},{256,384},{1,129},{129,257},{257,385},{2,130},{1... | collective-permute-start | bytes 1474568 | tf_op jit(solution)/shard_map/ppermute | solution.py:30
  516.0 13.9 %conditional.10 = ((f32[2,320,320]{2,1,0:T(8,128)}, f32[2,320,64]{1,2,0:T(8,128)}, f32[320,384]{1,0:T(8,128)})) conditional(s32[]{:T(128)} %convert_element_type.24, (f32[2,320,320]{2,1,0:T(8,128)}, f32[2,320,64]{1,2,0:T(8,128)}, f32[320,384]{1,0:T(8,128)}) %get-tuple-element.2896, (f32[320,384]{1,0:T(8,128)}, f32[2,320]{1,0:T(2,128)S(1)}, ...), branch_computations={%region_16.20_spmd, %region_17.23_spmd} | conditional | flops 895697216 | bytes 27820244 | solution.py:166
  541.3 223.1 %collective-permute-done.7 = f32[320,64]{0,1:T(8,128)S(1)} collective-permute-done((f32[320,64]{0,1:T(8,128)}, f32[320,64]{0,1:T(8,128)S(1)}, u32[]{:S(2)}, u32[]{:S(2)}) %collective-permute-start.7) | collective-permute-done | bytes 81952 | tf_op jit(solution)/shard_map/ppermute | solution.py:30
  772.6 461.9 %collective-permute-done.9 = f32[320,64]{0,1:T(8,128)S(1)} collective-permute-done((f32[320,64]{0,1:T(8,128)}, f32[320,64]{0,1:T(8,128)S(1)}, u32[]{:S(2)}, u32[]{:S(2)}) %collective-permute-start.9) | collective-permute-done | bytes 81952 | tf_op jit(solution)/shard_map/ppermute | solution.py:30
  1234.4 86.1 %conditional.15 = (f32[2,320,64]{1,2,0:T(8,128)}) conditional(s32[]{:T(128)} %convert_element_type.22, f32[2,320,64]{1,2,0:T(8,128)} %get-tuple-element.1022, (s32[2]{0:T(128)}, f32[3,320,320]{2,1,0:T(8,128)S(1)}, f32[2,320,320]{2,1,0:T(8,128)}, f32[2,320,64]{1,2,0:T(8,128)}, f32[320,64]{0,1:T(8,128)S(1)}) %tuple.611), branch_computations={%region_36.41_spmd, %region_37.44_spmd} | conditional | flops 186073088 | bytes 4186592 | solution.py:182
  1235.3 85.2 %while.184 = (s32[]{:T(128)}, f32[320,64]{0,1:T(8,128)S(1)}, f32[2,320,64]{1,2,0:T(8,128)}, s32[2]{0:T(128)}, f32[3,320,320]{2,1,0:T(8,128)S(1)}, /*index=5*/f32...) while((s32[]{:T(128)}, f32[320,64]{0,1:T(8,128)S(1)}, ...), condition=%wide.region_39.43_spmd, body=%wide.region_38.42_spmd.sunk | while | flops 186073088 | bytes 4022644 | solution.py:88
  1240.7 29.5 %custom-call.115 = f32[3,128,128]{1,2,0:T(8,128)S(1)} custom-call(f32[3,128,128]{2,1,0:T(8,128)S(1)} %pad_maximum_fusion.49), custom_call_target="InvertDiagBlocksLowerTriangular" | custom-call | tf_op jit(solution)/shard_map/cond/branch_1_fun/while/body/eval_jaxpr/jit(_solve_triangular)/triangular_solve | solution.py:38
  1283.3 29.5 %custom-call.115 = f32[3,128,128]{1,2,0:T(8,128)S(1)} custom-call(f32[3,128,128]{2,1,0:T(8,128)S(1)} %pad_maximum_fusion.49), custom_call_target="InvertDiagBlocksLowerTriangular" | custom-call | tf_op jit(solution)/shard_map/cond/branch_1_fun/while/body/eval_jaxpr/jit(_solve_triangular)/triangular_solve | solution.py:38
  (225 shorter events, 155.6 us)
Async XLA Ops:
  0.0 31.2 %copy-start = (f32[8,320]{1,0:T(8,128)S(1)}, f32[8,320]{1,0:T(8,128)}, u32[]{:S(2)}) copy-start(f32[8,320]{1,0:T(8,128)} %param.53) | copy-start | bytes 30724
  0.0 29.7 %copy-start.11 = (s32[1,1,2,2]{3,2,1,0:T(2,128)S(1)}, s32[1,1,2,2]{3,2,1,0:T(2,128)}, u32[]{:S(2)}) copy-start(s32[1,1,2,2]{3,2,1,0:T(2,128)} %param.57) | copy-start | bytes 52
  0.0 31.2 %copy-start.18 = (s32[1,1,2]{2,1,0:T(1,128)S(1)}, s32[1,1,2]{2,1,0:T(1,128)}, u32[]{:S(2)}) copy-start(s32[1,1,2]{2,1,0:T(1,128)} %param.56) | copy-start | bytes 28
  0.0 13.7 %collective-permute-start = (f32[1,1,2,64,320]{4,3,2,1,0:T(8,128)}, f32[1,1,2,64,320]{4,3,2,1,0:T(8,128)S(1)}, u32[]{:S(2)}, u32[]{:S(2)}) collective-permute-start(f32[1,1,2,64,320]{4,3,2,1,0:T(8,128)} %param.52), channel_id=1, source_target_pairs={{0,8},{8,16},{16,24},{24,32},{32,40},{40,48},{48,56},{56,64},{64,7... | collective-permute-start | bytes 491528 | tf_op jit(solution)/shard_map/ppermute | solution.py:18
  5.1 11.6 collective-permute-start.1
  16.7 23.7 %collective-permute-start.3 = (f32[3,1,2,64,320]{4,3,2,1,0:T(8,128)S(1)}, f32[3,1,2,64,320]{4,3,2,1,0:T(8,128)S(1)}, u32[]{:S(2)}, u32[]{:S(2)}) collective-permute-start(f32[3,1,2,64,320]{4,3,2,1,0:T(8,128)S(1)} %constant_dynamic-update-slice_fusion.12), channel_id=1, source_target_pairs={{1,0},{2,1},{3,2},{4,3},{5,4},{6,5},{7,6},{0,7},{9,8},{10,9},{11,1... | collective-permute-start | bytes 1474568 | tf_op jit(solution)/shard_map/ppermute | solution.py:20
  27.7 19.0 %copy-start.2 = (f32[320,320]{1,0:T(8,128)}, f32[320,320]{1,0:T(8,128)S(1)}, u32[]{:S(2)}) copy-start(f32[320,320]{1,0:T(8,128)S(1)} %fusion.260) | copy-start | bytes 1228804
  27.7 18.1 %collective-permute-start.2 = (f32[3,1,2,64,320]{4,3,2,1,0:T(8,128)S(1)}, f32[3,1,2,64,320]{4,3,2,1,0:T(8,128)S(1)}, u32[]{:S(2)}, u32[]{:S(2)}) collective-permute-start(f32[3,1,2,64,320]{4,3,2,1,0:T(8,128)S(1)} %constant_dynamic-update-slice_fusion.12), channel_id=1, source_target_pairs={{0,1},{1,2},{2,3},{3,4},{4,5},{5,6},{6,7},{7,0},{8,9},{9,10},{10,1... | collective-permute-start | bytes 1474568 | tf_op jit(solution)/shard_map/ppermute | solution.py:18
  30.4 256.3 %copy-start.12 = (s32[2]{0:T(128)}, s32[2]{0:T(128)S(1)}, u32[]{:S(2)}) copy-start(s32[2]{0:T(128)S(1)} %get-tuple-element.1226) | copy-start | bytes 28
  30.4 16.4 %copy-start.17 = (s32[1,1,2,4]{3,2,1,0:T(2,128)S(1)}, s32[1,1,2,4]{3,2,1,0:T(2,128)}, u32[]{:S(2)}) copy-start(s32[1,1,2,4]{3,2,1,0:T(2,128)} %param.58) | copy-start | bytes 100
  46.8 13.2 copy-start.1
  59.9 1.7 copy-start.3
  283.7 3.0 collective-permute-start.4
  300.7 215.3 %collective-permute-start.5 = (f32[320,384]{1,0:T(8,128)}, f32[320,384]{1,0:T(8,128)}, u32[]{:S(2)}, u32[]{:S(2)}) collective-permute-start(f32[320,384]{1,0:T(8,128)} %get-tuple-element.1013), channel_id=1, source_target_pairs={{0,128},{128,256},{256,384},{1,129},{129,257},{257,385},{2,130},{1... | collective-permute-start | bytes 1474568 | tf_op jit(solution)/shard_map/ppermute | solution.py:30
  530.0 8.0 collective-permute-start.6
  540.0 224.3 %collective-permute-start.7 = (f32[320,64]{0,1:T(8,128)}, f32[320,64]{0,1:T(8,128)S(1)}, u32[]{:S(2)}, u32[]{:S(2)}) collective-permute-start(f32[320,64]{0,1:T(8,128)} %get-tuple-element.1019), channel_id=1, source_target_pairs={{128,0},{256,128},{384,256},{129,1},{257,129},{385,257},{130,2},{2... | collective-permute-start | bytes 245768 | tf_op jit(solution)/shard_map/ppermute | solution.py:30
  764.4 6.9 collective-permute-start.8
  771.3 463.2 %collective-permute-start.9 = (f32[320,64]{0,1:T(8,128)}, f32[320,64]{0,1:T(8,128)S(1)}, u32[]{:S(2)}, u32[]{:S(2)}) collective-permute-start(f32[320,64]{0,1:T(8,128)} %get-tuple-element.1023), channel_id=1, source_target_pairs={{128,0},{256,128},{384,256},{129,1},{257,129},{385,257},{130,2},{2... | collective-permute-start | bytes 245768 | tf_op jit(solution)/shard_map/ppermute | solution.py:30
where the time goes:
time: 1330 us; the launch traced here: 1320 us
  waiting for transfers between devices  715 us (54%)
  starting transfers between devices  249 us (19%)
  other arithmetic  230 us (17%)
  loops' own time  59.4 us (4%)
  local copies, waits for them, and re-layouts  37.2 us (3%)
  matrix products  30.2 us (2%)
    ppermute x6, waiting for transfers between devices, from_behind(): return lax.ppermute(value, axis, pairs)  694 us
    ppermute x6, starting transfers between devices, from_behind(): return lax.ppermute(value, axis, pairs)  226 us
    another operation x20, other arithmetic, advance_one(): factor = jnp.linalg.cholesky(pivot_now)  101 us
    another operation x16, other arithmetic, upper_solve(): jax.scipy.linalg.solve_triangular(factor, values, lower=True, trans=1)  61.4 us
    another operation x16, other arithmetic, lower_solve(): return jax.scipy.linalg.solve_triangular(factor, values, lower=True)  59.3 us
    another operation x4, loops' own time, on_device(): lax.cond(wall_position == section_number, advance, keep_state, section_st...  42.8 us
  transfers between devices with their start and end apart: 10, of which 10 were waited for; matrix products, arithmetic and copies ran while one was open for 0% of the time, Pallas kernels for 0%

commit v1 on v0

v1 whole, which is shorter than its diff:
```python
import jax
import jax.numpy as jnp
from jax import lax
from jax.sharding import PartitionSpec as P

HIGHEST = lax.Precision.HIGHEST


def padded_2(cells, sides, width):
    for axis, dim in sides:
        count = lax.axis_size(axis)
        head = lax.slice_in_dim(cells, 0, width, axis=dim)
        tail = lax.slice_in_dim(cells, cells.shape[dim] - width, cells.shape[dim], axis=dim)
        cells = jnp.concatenate(
            [
                lax.ppermute(tail, axis, [(i, (i + 1) % count) for i in range(count)]),
                cells,
                lax.ppermute(head, axis, [((i + 1) % count, i) for i in range(count)]),
            ],
            axis=dim,
        )
    return cells


def mm(spec, a, b):
    return jnp.einsum(spec, a, b, precision=HIGHEST)


def tr(a):
    return jnp.swapaxes(a, -1, -2)


def inverse_spd(blocks):
    factor = jnp.linalg.cholesky(blocks)
    eye = jnp.broadcast_to(jnp.eye(blocks.shape[-1], dtype=blocks.dtype), blocks.shape)
    factor_inv = lax.linalg.triangular_solve(factor, eye, left_side=True, lower=True)
    return mm("bki,bkj->bij", factor_inv, factor_inv)


def factor_line(diag, upper):
    levels = []
    while diag.shape[0] > 1:
        count = diag.shape[0]
        odd_count = count // 2
        has_right = [2 * j + 2 < count for j in range(odd_count)]
        right_count = sum(has_right)
        inv_odd = inverse_spd(diag[1::2])
        left = upper[0::2][:odd_count]
        right = upper[1::2][:right_count]
        to_left = mm("bij,bkj->bik", inv_odd, left)
        to_right = mm("bij,bjk->bik", inv_odd[:right_count], right)
        even = diag[0::2]
        even_count = even.shape[0]
        first = mm("bij,bjk->bik", left, to_left)
        even = even.at[:odd_count].add(-first)
        second = mm("bji,bjk->bik", right, to_right)
        even = even.at[1 : 1 + right_count].add(-second)
        next_upper = mm("bij,bjk->bik", left[: even_count - 1], to_right[: even_count - 1])
        levels.append((inv_odd, to_left, to_right))
        diag, upper = even, next_upper
    last_inv = inverse_spd(diag)
    return levels, last_inv


def solve_line(levels, last_inv, rhs):
    kept = []
    for inv_odd, to_left, to_right in levels:
        count = rhs.shape[0]
        odd = rhs[1::2]
        even = rhs[0::2]
        odd_count = odd.shape[0]
        right_count = to_right.shape[0]
        even = even.at[:odd_count].add(mm("bji,bjv->biv", to_left, odd))
        even = even.at[1 : 1 + right_count].add(mm("bji,bjv->biv", to_right, odd[:right_count]))
        kept.append((odd, count))
        rhs = even
    values = mm("bij,bjv->biv", last_inv, rhs)
    for (inv_odd, to_left, to_right), (odd, count) in zip(reversed(levels), reversed(kept)):
        right_count = to_right.shape[0]
        odd_values = mm("bij,bjv->biv", inv_odd, odd)
        odd_values = odd_values + mm("bij,bjv->biv", to_left, values[: odd.shape[0]])
        odd_values = odd_values.at[:right_count].add(
            mm("bij,bjv->biv", to_right, values[1 : 1 + right_count])
        )
        merged = jnp.zeros((count,) + values.shape[1:], values.dtype)
        merged = merged.at[0::2].set(values).at[1::2].set(odd_values)
        values = merged
    return values


def on_device(
    right_side,
    old_values,
    element_library,
    wall_library,
    face_library,
    element_index,
    wall_faces,
    face_index,
):
    local_side = right_side[0, 0]
    element_count = local_side.shape[0]
    indices = jnp.concatenate([element_index[0, 0][:, None], wall_faces[0, 0]], axis=1)
    line_indices = lax.all_gather(indices, "wall", axis=0, tiled=True)
    rates = element_library[line_indices[:, 0]]
    below = wall_library[line_indices[:, 1]]
    above = wall_library[line_indices[:, 2]]
    unknowns = rates.shape[1]
    diag = below + above + rates[:, :, None] * jnp.eye(unknowns, dtype=rates.dtype)[None]
    levels, last_inv = factor_line(diag, below[1:])

    padded = padded_2(old_values, (("span", 0), ("stream", 1)), 1)
    near_rows = jnp.stack([padded[0, 1], padded[2, 1], padded[1, 0], padded[1, 2]], axis=1)
    blocks = face_library[face_index[0, 0]]
    coupled = mm("edjk,edvk->ejv", blocks, near_rows)
    residual_t = jnp.swapaxes(local_side, 1, 2) - coupled
    line_residual = lax.all_gather(residual_t, "wall", axis=0, tiled=True)

    line_values = solve_line(levels, last_inv, line_residual)
    start = lax.axis_index("wall") * element_count
    own = lax.dynamic_slice_in_dim(line_values, start, element_count, axis=0)
    return jnp.swapaxes(own, 1, 2)[None, None]


def solution(mesh):
    placed = (
        P("span", "stream", "wall", None, None),
        P("span", "stream", "wall", None, None),
        P(),
        P(),
        P(),
        P("span", "stream", "wall"),
        P("span", "stream", "wall", None),
        P("span", "stream", "wall", None),
    )
    return jax.shard_map(
        on_device,
        mesh=mesh,
        in_specs=placed,
        out_specs=P("span", "stream", "wall", None, None),
        check_vma=False,
    )
```

time: 1330 us -> 983 us (0.74)
  the two profiles are of different devices: /device:TPU:32 before, /device:TPU:1 now
where the time goes in v1:
time: 983 us; the launch traced here: 972 us
  other arithmetic  689 us (70%)
  matrix products  122 us (12%)
  local copies, waits for them, and re-layouts  108 us (11%)
  blocking collectives  20.4 us (2%)
  starting transfers between devices  18.3 us (2%)
    another operation x48, other arithmetic, inverse_spd(): factor = jnp.linalg.cholesky(blocks)  423 us
    another operation x20, other arithmetic, inverse_spd(): lax.linalg.triangular_solve(factor, eye, left_side=True, lower=True)  251 us
    dot_general x31, matrix products, mm(): return jnp.einsum(spec, a, b, precision=HIGHEST)  72.1 us
    another operation x20, matrix products, inverse_spd(): lax.linalg.triangular_solve(factor, eye, left_side=True, lower=True)  27.1 us
    another operation x16, matrix products, inverse_spd(): factor = jnp.linalg.cholesky(blocks)  22.6 us
    unnamed x128, local copies, waits for them, and re-layouts  20.3 us
  transfers between devices with their start and end apart: 4, of which 2 were waited for; matrix products, arithmetic and copies ran while one was open for 90% of the time, Pallas kernels for 0%

profile of v1, /device:TPU:1, one launch (start us, length us, event | category | flops | bytes accessed | tf_op | source)
XLA Modules:
  0.0 971.6 jit_solution(8845997995729289194)
XLA Ops:
  15.4 10.9 %all-gather = s32[4,2,3]{2,1,0:T(2,128)S(1)} all-gather(s32[1,2,3]{2,1,0:T(2,128)S(1)} %add_bitcast_fusion), channel_id=1, replica_groups=mesh['wall'=4,'span'=16,'stream'=8] {'wall'}, dimensions={0}, use_global_device_ids=true | all-gather | bytes 120 | tf_op jit(solution)/shard_map/all_gather | solution.py:104
  62.6 46.9 %custom-call.70 = f32[4,128,128]{2,1,0:T(8,128)S(1)} custom-call(f32[4,128,128]{2,1,0:T(8,128)S(1)} %copy.168), custom_call_target="Cholesky" | custom-call | tf_op jit(solution)/shard_map/jit(cholesky)/cholesky | solution.py:34
  109.5 39.3 %custom-call.71 = f32[4,1,128,128]{2,3,1,0:T(8,128)S(1)} custom-call(f32[4,1,128,128]{3,2,1,0:T(8,128)S(1)} %select_bitcast_fusion.1), custom_call_target="InvertDiagBlocksLowerTriangular" | custom-call | tf_op jit(solution)/shard_map/jit(cholesky)/cholesky | solution.py:34
  154.0 47.1 %custom-call.72 = f32[4,128,128]{2,1,0:T(8,128)S(1)} custom-call(f32[4,128,128]{2,1,0:T(8,128)S(1)} %copy.173), custom_call_target="Cholesky" | custom-call | tf_op jit(solution)/shard_map/jit(cholesky)/cholesky | solution.py:34
  201.8 39.3 %custom-call.73 = f32[4,1,128,128]{2,3,1,0:T(8,128)S(1)} custom-call(f32[4,1,128,128]{3,2,1,0:T(8,128)S(1)} %get-tuple-element.304), custom_call_target="InvertDiagBlocksLowerTriangular" | custom-call | tf_op jit(solution)/shard_map/jit(cholesky)/cholesky | solution.py:34
  244.0 23.5 %custom-call.74 = f32[4,64,64]{2,1,0:T(8,128)S(1)} custom-call(f32[4,64,64]{2,1,0:T(8,128)S(1)} %copy.177), custom_call_target="Cholesky" | custom-call | tf_op jit(solution)/shard_map/jit(cholesky)/cholesky | solution.py:34
  280.2 119.5 %custom-call.75 = f32[4,3,128,128]{2,3,1,0:T(8,128)} custom-call(f32[4,3,128,128]{3,2,1,0:T(8,128)} %pad_maximum_fusion), custom_call_target="InvertDiagBlocksLowerTriangular" | custom-call | tf_op jit(solution)/shard_map/triangular_solve | solution.py:36
  446.4 23.5 %custom-call.76 = f32[2,128,128]{2,1,0:T(8,128)S(1)} custom-call(f32[2,128,128]{2,1,0:T(8,128)S(1)} %copy.189), custom_call_target="Cholesky" | custom-call | tf_op jit(solution)/shard_map/jit(cholesky)/cholesky | solution.py:34
  470.0 19.7 %custom-call.77 = f32[2,1,128,128]{2,3,1,0:T(8,128)S(1)} custom-call(f32[2,1,128,128]{3,2,1,0:T(8,128)S(1)} %select_bitcast_fusion.3), custom_call_target="InvertDiagBlocksLowerTriangular" | custom-call | tf_op jit(solution)/shard_map/jit(cholesky)/cholesky | solution.py:34
  495.1 25.1 %custom-call.78 = f32[2,128,128]{2,1,0:T(8,128)} custom-call(f32[2,128,128]{2,1,0:T(8,128)} %copy.194), custom_call_target="Cholesky" | custom-call | tf_op jit(solution)/shard_map/jit(cholesky)/cholesky | solution.py:34
  522.4 20.5 %custom-call.79 = f32[2,1,128,128]{2,3,1,0:T(8,128)S(1)} custom-call(f32[2,1,128,128]{3,2,1,0:T(8,128)} %get-tuple-element.306), custom_call_target="InvertDiagBlocksLowerTriangular" | custom-call | tf_op jit(solution)/shard_map/jit(cholesky)/cholesky | solution.py:34
  544.5 11.7 %custom-call.80 = f32[2,64,64]{2,1,0:T(8,128)S(1)} custom-call(f32[2,64,64]{2,1,0:T(8,128)S(1)} %copy.198), custom_call_target="Cholesky" | custom-call | tf_op jit(solution)/shard_map/jit(cholesky)/cholesky | solution.py:34
  566.5 59.4 %custom-call.81 = f32[2,3,128,128]{2,3,1,0:T(8,128)S(1)} custom-call(f32[2,3,128,128]{3,2,1,0:T(8,128)S(1)} %pad_maximum_fusion.1), custom_call_target="InvertDiagBlocksLowerTriangular" | custom-call | tf_op jit(solution)/shard_map/triangular_solve | solution.py:36
  652.3 12.5 %custom-call.88 = f32[1,128,128]{2,1,0:T(8,128)S(1)} custom-call(f32[1,128,128]{2,1,0:T(8,128)} %cholesky.739), custom_call_target="Cholesky" | custom-call | tf_op jit(solution)/shard_map/jit(cholesky)/cholesky | solution.py:34
  667.8 11.3 %custom-call.89 = f32[1,1,128,128]{2,3,1,0:T(8,128)} custom-call(f32[1,1,128,128]{3,2,1,0:T(8,128)} %get-tuple-element.319), custom_call_target="InvertDiagBlocksLowerTriangular" | custom-call | tf_op jit(solution)/shard_map/jit(cholesky)/cholesky | solution.py:34
  683.3 13.2 %custom-call.90 = f32[1,128,128]{2,1,0:T(8,128)} custom-call(f32[1,128,128]{2,1,0:T(8,128)} %cholesky.743), custom_call_target="Cholesky" | custom-call | tf_op jit(solution)/shard_map/jit(cholesky)/cholesky | solution.py:34
  699.3 11.6 %custom-call.91 = f32[1,1,128,128]{2,3,1,0:T(8,128)} custom-call(f32[1,1,128,128]{3,2,1,0:T(8,128)} %get-tuple-element.316), custom_call_target="InvertDiagBlocksLowerTriangular" | custom-call | tf_op jit(solution)/shard_map/jit(cholesky)/cholesky | solution.py:34
  734.7 30.9 %custom-call.93 = f32[1,3,128,128]{2,3,1,0:T(8,128)} custom-call(f32[1,3,128,128]{3,2,1,0:T(8,128)} %pad_maximum_fusion.2), custom_call_target="InvertDiagBlocksLowerTriangular" | custom-call | tf_op jit(solution)/shard_map/triangular_solve/custom-call.17 | solution.py:36
  782.4 13.2 %custom-call.94 = f32[1,128,128]{2,1,0:T(8,128)} custom-call(f32[1,128,128]{2,1,0:T(8,128)} %cholesky.747), custom_call_target="Cholesky" | custom-call | tf_op jit(solution)/shard_map/jit(cholesky)/cholesky | solution.py:34
  798.8 11.3 %custom-call.95 = f32[1,1,128,128]{2,3,1,0:T(8,128)} custom-call(f32[1,1,128,128]{3,2,1,0:T(8,128)} %get-tuple-element.314), custom_call_target="InvertDiagBlocksLowerTriangular" | custom-call | tf_op jit(solution)/shard_map/jit(cholesky)/cholesky | solution.py:34
  814.2 13.3 %custom-call.96 = f32[1,128,128]{2,1,0:T(8,128)} custom-call(f32[1,128,128]{2,1,0:T(8,128)} %cholesky.751), custom_call_target="Cholesky" | custom-call | tf_op jit(solution)/shard_map/jit(cholesky)/cholesky | solution.py:34
  830.4 11.3 %custom-call.97 = f32[1,1,128,128]{2,3,1,0:T(8,128)} custom-call(f32[1,1,128,128]{3,2,1,0:T(8,128)} %get-tuple-element.311), custom_call_target="InvertDiagBlocksLowerTriangular" | custom-call | tf_op jit(solution)/shard_map/jit(cholesky)/cholesky | solution.py:34
  865.5 30.9 %custom-call.99 = f32[1,3,128,128]{2,3,1,0:T(8,128)} custom-call(f32[1,3,128,128]{3,2,1,0:T(8,128)} %pad_maximum_fusion.3), custom_call_target="InvertDiagBlocksLowerTriangular" | custom-call | tf_op jit(solution)/shard_map/triangular_solve/custom-call.17 | solution.py:36
  937.4 9.5 all_gather.7
  (356 shorter events, 338.0 us)
Async XLA Ops:
  0.0 914.9 %copy-start = (f32[4,320,320]{2,1,0:T(8,128)S(1)}, f32[4,320,320]{2,1,0:T(8,128)}, u32[]{:S(2)}) copy-start(f32[4,320,320]{2,1,0:T(8,128)} %param.55) | copy-start | bytes 4915204
  0.0 27.8 %copy-start.1 = (f32[3,320,320]{2,1,0:T(8,128)S(1)}, f32[3,320,320]{2,1,0:T(8,128)}, u32[]{:S(2)}) copy-start(f32[3,320,320]{2,1,0:T(8,128)} %param.54) | copy-start | bytes 3686404
  0.0 900.2 %collective-permute-start = (f32[1,1,2,64,320]{4,3,2,1,0:T(8,128)}, f32[1,1,2,64,320]{4,3,2,1,0:T(8,128)}, u32[]{:S(2)}, u32[]{:S(2)}) collective-permute-start(f32[1,1,2,64,320]{4,3,2,1,0:T(8,128)} %param.52), channel_id=1, source_target_pairs={{0,8},{8,16},{16,24},{24,32},{32,40},{40,48},{48,56},{56,64},{64,7... | collective-permute-start | bytes 491528 | tf_op jit(solution)/shard_map/ppermute | solution.py:16
  5.7 897.7 %collective-permute-start.1 = (f32[1,1,2,64,320]{4,3,2,1,0:T(8,128)}, f32[1,1,2,64,320]{4,3,2,1,0:T(8,128)}, u32[]{:S(2)}, u32[]{:S(2)}) collective-permute-start(f32[1,1,2,64,320]{4,3,2,1,0:T(8,128)} %param.52), channel_id=1, source_target_pairs={{8,0},{16,8},{24,16},{32,24},{40,32},{48,40},{56,48},{64,56},{72,6... | collective-permute-start | bytes 491528 | tf_op jit(solution)/shard_map/ppermute | solution.py:18
  11.4 189.6 %copy-start.57 = (pred[128,128]{1,0:T(8,128)(4,1)}, pred[128,128]{1,0:T(8,128)(4,1)S(1)}, u32[]{:S(2)}) copy-start(pred[128,128]{1,0:T(8,128)(4,1)S(1)} %get-tuple-element.343) | copy-start | bytes 49156
  11.5 256.0 %copy-start.59 = (pred[64,64]{1,0:T(8,128)(4,1)}, pred[64,64]{1,0:T(8,128)(4,1)S(1)}, u32[]{:S(2)}) copy-start(pred[64,64]{1,0:T(8,128)(4,1)S(1)} %iota_compare_fusion.13) | copy-start | bytes 12292
  153.8 114.7 %copy-start.43 = (pred[320,320]{1,0:T(8,128)(4,1)S(1)}, pred[320,320]{1,0:T(8,128)(4,1)}, u32[]{:S(2)}) copy-start(pred[320,320]{1,0:T(8,128)(4,1)} %iota_compare_fusion.2) | copy-start | bytes 307204
  278.0 125.1 %copy-start.61 = (s32[2,2]{1,0:T(2,128)}, s32[2,2]{1,0:T(2,128)S(1)}, u32[]{:S(2)}) copy-start(s32[2,2]{1,0:T(2,128)S(1)} %get-tuple-element.526) | copy-start | bytes 52
  278.0 121.8 %copy-start.36 = (f32[128,320]{0,1:T(8,128)S(1)}, f32[128,320]{0,1:T(8,128)}, u32[]{:S(2)}) copy-start(f32[128,320]{0,1:T(8,128)} %get-tuple-element.303) | copy-start | bytes 491524
  278.0 123.4 %copy-start.39 = (f32[128,320]{0,1:T(8,128)S(1)}, f32[128,320]{0,1:T(8,128)}, u32[]{:S(2)}) copy-start(f32[128,320]{0,1:T(8,128)} %get-tuple-element.302) | copy-start | bytes 491524
  446.3 73.8 %copy-start.58 = (pred[128,128]{1,0:T(8,128)(4,1)S(1)}, pred[128,128]{1,0:T(8,128)(4,1)}, u32[]{:S(2)}) copy-start(pred[128,128]{1,0:T(8,128)(4,1)} %copy-done.57) | copy-start | bytes 49156
  470.0 86.2 %copy-start.60 = (pred[64,64]{1,0:T(8,128)(4,1)S(1)}, pred[64,64]{1,0:T(8,128)(4,1)}, u32[]{:S(2)}) copy-start(pred[64,64]{1,0:T(8,128)(4,1)} %copy-done.59) | copy-start | bytes 12292
  470.0 88.0 %copy-start.44 = (pred[320,320]{1,0:T(8,128)(4,1)S(1)}, pred[320,320]{1,0:T(8,128)(4,1)}, u32[]{:S(2)}) copy-start(pred[320,320]{1,0:T(8,128)(4,1)} %iota_compare_fusion.2) | copy-start | bytes 307204
  543.2 15.9 %copy-start.54 = (f32[2,2,128,128]{3,2,0,1:T(8,128)S(1)}, f32[2,2,128,128]{3,2,0,1:T(8,128)}, u32[]{:S(2)}) copy-start(f32[2,2,128,128]{3,2,0,1:T(8,128)} %custom-call.110) | copy-start | bytes 786436
  544.4 21.9 %copy-start.49 = (f32[128,64]{1,0:T(8,128)S(1)}, f32[128,64]{1,0:T(8,128)}, u32[]{:S(2)}) copy-start(f32[128,64]{1,0:T(8,128)} %copy-done.48) | copy-start | bytes 98308
  558.2 67.7 %copy-start.37 = (f32[128,320]{0,1:T(8,128)S(1)}, f32[128,320]{0,1:T(8,128)}, u32[]{:S(2)}) copy-start(f32[128,320]{0,1:T(8,128)} %get-tuple-element.303) | copy-start | bytes 491524
  558.2 68.1 %copy-start.40 = (f32[128,320]{0,1:T(8,128)S(1)}, f32[128,320]{0,1:T(8,128)}, u32[]{:S(2)}) copy-start(f32[128,320]{0,1:T(8,128)} %get-tuple-element.302) | copy-start | bytes 491524
  566.3 61.8 %copy-start.46 = (f32[64,320]{1,0:T(8,128)S(1)}, f32[64,320]{1,0:T(8,128)}, u32[]{:S(2)}) copy-start(f32[64,320]{1,0:T(8,128)} %copy-done.45) | copy-start | bytes 245764
  651.7 74.4 %copy-start.62 = (s32[2,2]{1,0:T(2,128)S(1)}, s32[2,2]{1,0:T(2,128)}, u32[]{:S(2)}) copy-start(s32[2,2]{1,0:T(2,128)} %get-tuple-element.527) | copy-start | bytes 52
  666.1 66.9 %copy-start.50 = (f32[1,128,64]{2,1,0:T(8,128)S(1)}, f32[1,128,64]{2,1,0:T(8,128)}, u32[]{:S(2)}) copy-start(f32[1,128,64]{2,1,0:T(8,128)} %get-tuple-element.326) | copy-start | bytes 98308
  905.1 18.4 %collective-permute-start.3 = (f32[3,1,2,64,320]{4,3,2,1,0:T(8,128)}, f32[3,1,2,64,320]{4,3,2,1,0:T(8,128)}, u32[]{:S(2)}, u32[]{:S(2)}) collective-permute-start(f32[3,1,2,64,320]{4,3,2,1,0:T(8,128)} %constant_dynamic-update-slice_fusion), channel_id=1, source_target_pairs={{1,0},{2,1},{3,2},{4,3},{5,4},{6,5},{7,6},{0,7},{9,8},{10,9},{11,1... | collective-permute-start | bytes 1474568 | tf_op jit(solution)/shard_map/ppermute | solution.py:18
  912.7 17.8 %collective-permute-start.2 = (f32[3,1,2,64,320]{4,3,2,1,0:T(8,128)}, f32[3,1,2,64,320]{4,3,2,1,0:T(8,128)}, u32[]{:S(2)}, u32[]{:S(2)}) collective-permute-start(f32[3,1,2,64,320]{4,3,2,1,0:T(8,128)} %constant_dynamic-update-slice_fusion), channel_id=1, source_target_pairs={{0,1},{1,2},{2,3},{3,4},{4,5},{5,6},{6,7},{7,0},{8,9},{9,10},{10,1... | collective-permute-start | bytes 1474568 | tf_op jit(solution)/shard_map/ppermute | solution.py:16
  917.7 13.8 %copy-start.56 = (f32[1,1,2,64,320]{4,3,2,1,0:T(8,128)S(1)}, f32[1,1,2,64,320]{4,3,2,1,0:T(8,128)}, u32[]{:S(2)}) copy-start(f32[1,1,2,64,320]{4,3,2,1,0:T(8,128)} %param.51) | copy-start | bytes 491524
  931.5 15.4 %copy-start.2 = (f32[4,320,320]{2,1,0:T(8,128)S(1)}, f32[4,320,320]{2,1,0:T(8,128)}, u32[]{:S(2)}) copy-start(f32[4,320,320]{2,1,0:T(8,128)} %fusion.11) | copy-start | bytes 4915204
  (44 other events, 148.2 us)
